TPU v7x, 256 devices: a whole 4x4x8 slice. The times are simulated.
256 devices in a mesh: group: 2 (over core), dp: 16 (over y, x), tensor: 8 (over z).
Axes of the slice: x: 4, y: 4, z: 8, core: 2. Of those that a mesh axis runs over, the one named last changes fastest.
Arguments:
- stream: bfloat16 [512, 8192], P('tensor', ('group', 'dp'))
- norm_attn: bfloat16 [8192], P(('group', 'dp')), may hold values from 0.29882812 to 3
- norm_ffn: bfloat16 [8192], P(('group', 'dp')), may hold values from 0.29882812 to 3
- w_query: bfloat16 [8192, 8192], P(('group', 'dp'), 'tensor'), may hold values from -0.0625 to 0.0625
- w_keyval: bfloat16 [8192, 2048], P(('group', 'dp'), 'tensor'), may hold values from -0.0625 to 0.0625
- w_out: bfloat16 [8192, 8192], P('tensor', ('group', 'dp')), may hold values from -0.0625 to 0.0625
- w_gate: bfloat16 [8192, 28672], P(('group', 'dp'), 'tensor'), may hold values from -0.0625 to 0.0625
- w_up: bfloat16 [8192, 28672], P(('group', 'dp'), 'tensor'), may hold values from -0.0625 to 0.0625
- w_down: bfloat16 [28672, 8192], P('tensor', ('group', 'dp')), may hold values from -0.03125 to 0.03125
- cache: bfloat16 [512, 8, 256, 256], P(('group', 'dp'), 'tensor')
- lengths: int32 [512], P(('group', 'dp')), may hold values from 1 to 256, as said below
- location: int32 [512], P(('group', 'dp')), may hold values from 0 to 511, as said below
Outputs:
- updated: float32 [512, 8192], P('tensor', ('group', 'dp'))
Inputs may be any that keep to these rules, and one draw needn't show every extreme that they name: Each of the 512 slots is named by exactly one request. Slot s belongs to owner s // 16. Requests r of one aligned block of 16 (one device's requests) that share an owner have different values of location modulo 2; in every draw 2 of them share an owner. `lengths`: some slot holds 256 valid positions in every draw.
All inputs are finite; a program needn't handle non-finite values.
Results may differ from a plain program's by a relative error of at most 0.005.
The roundings to bfloat16 on the way count: a program that leaves them out, or rounds other values in their place, can miss the bound.
Values may be sent and summed in bfloat16 or wider, within the bound.
No kernel may reach another device: no remote copies, remote signals or barrier semaphores. Data moves between devices by JAX's collectives and lax.ppermute only.
A program may use at most 64 MiB of HBM per device.

v0:
```python
import jax
import jax.numpy as jnp
from jax import lax
from jax.sharding import PartitionSpec as P

D = 8192
CAP = 2
EPSILON = 1e-05


def normed(values, gain):
    squares = lax.psum(jnp.sum(values * values, axis=1), ("group", "dp"))
    scale = lax.rsqrt(squares / D + EPSILON)
    return (values * scale[:, None] * gain.astype(jnp.float32)[None, :]).astype(jnp.bfloat16)


def width_sum(normal_rows, matrices):
    gathered = lax.all_gather(normal_rows, "tensor", axis=0, tiled=True)
    return lax.psum_scatter(
        jnp.concatenate(
            [jnp.dot(gathered, matrix, preferred_element_type=jnp.float32) for matrix in matrices],
            axis=1,
        ),
        ("group", "dp"),
        scatter_dimension=0,
        tiled=True,
    )


def project_rows(local_rows, matrix):
    partial_sum = jnp.dot(
        lax.all_gather(local_rows, ("group", "dp"), axis=0, tiled=True),
        matrix,
        preferred_element_type=jnp.float32,
    )
    return lax.psum_scatter(partial_sum, "tensor", scatter_dimension=0, tiled=True)


def attend(query, fresh, stored, counts):
    items = query.shape[0]
    kv_local = stored.shape[1]
    head_size = stored.shape[3] // 2
    grouped = query.reshape(items, kv_local, -1, head_size)
    fresh = fresh.reshape(items, kv_local, 2 * head_size)
    scale = head_size ** (-0.5)
    scores = (
        jnp.einsum(
            "mkgd,mkpd->mkgp", grouped, stored[..., :head_size], preferred_element_type=jnp.float32
        )
        * scale
    )
    own = (
        jnp.einsum(
            "mkgd,mkd->mkg", grouped, fresh[..., :head_size], preferred_element_type=jnp.float32
        )
        * scale
    )
    place = jnp.arange(stored.shape[2], dtype=jnp.int32)
    valid = place[None, None, None, :] < counts[:, None, None, None]
    top = jnp.maximum(jnp.max(jnp.where(valid, scores, -1e30), axis=3), own)
    expo = jnp.where(valid, jnp.exp(scores - top[..., None]), 0.0)
    own_expo = jnp.exp(own - top)
    total = jnp.sum(expo, axis=3) + own_expo
    probs = (expo / total[..., None]).astype(jnp.bfloat16)
    own_prob = (own_expo / total).astype(jnp.bfloat16)
    mixed = jnp.einsum(
        "mkgp,mkpd->mkgd", probs, stored[..., head_size:], preferred_element_type=jnp.float32
    )
    mixed = mixed + own_prob.astype(jnp.float32)[..., None] * fresh[:, :, None, head_size:].astype(
        jnp.float32
    )
    return mixed.reshape(items, -1).astype(jnp.bfloat16)


def per_device(
    stream,
    norm_attn,
    norm_ffn,
    w_query,
    w_keyval,
    w_out,
    w_gate,
    w_up,
    w_down,
    cache,
    lengths,
    location,
):
    owners = lax.axis_size(("group", "dp"))
    per_owner = cache.shape[0]
    resid = stream.astype(jnp.float32)
    attn_in = normed(resid, norm_attn)
    joined = width_sum(attn_in, (w_query, w_keyval))
    query_cols = w_query.shape[1]
    query = joined[:, :query_cols].astype(jnp.bfloat16)
    fresh = joined[:, query_cols:].astype(jnp.bfloat16)
    fresh_cols = fresh.shape[1]
    target = location // per_owner
    place = target * CAP + location % per_owner % CAP
    slot = location % per_owner
    send_query = (
        jnp.zeros((owners * CAP, query_cols), jnp.bfloat16)
        .at[place]
        .set(query)
        .reshape(owners, CAP, query_cols)
    )
    send_fresh = (
        jnp.zeros((owners * CAP, fresh_cols), jnp.bfloat16)
        .at[place]
        .set(fresh)
        .reshape(owners, CAP, fresh_cols)
    )
    send_slot = jnp.zeros((owners * CAP,), jnp.int32).at[place].set(slot).reshape(owners, CAP)
    got_query = lax.all_to_all(send_query, ("group", "dp"), split_axis=0, concat_axis=0, tiled=True)
    got_fresh = lax.all_to_all(send_fresh, ("group", "dp"), split_axis=0, concat_axis=0, tiled=True)
    got_slot = lax.all_to_all(send_slot, ("group", "dp"), split_axis=0, concat_axis=0, tiled=True)
    sources = got_slot.shape[0]
    count = got_slot.shape[1]
    flat_slot = got_slot.reshape(-1)
    answer = attend(
        got_query.reshape(sources * count, -1),
        got_fresh.reshape(sources * count, -1),
        cache[flat_slot],
        lengths[flat_slot],
    )
    answer = answer.reshape(sources, count, -1)
    returned = lax.all_to_all(answer, ("group", "dp"), split_axis=0, concat_axis=0, tiled=True)
    attended = returned.reshape(owners * CAP, -1)[place]
    middle = resid + project_rows(attended, w_out)
    ffn_in = normed(middle, norm_ffn)
    both = width_sum(ffn_in, (w_gate, w_up))
    hidden_cols = w_gate.shape[1]
    hidden = (jax.nn.silu(both[:, :hidden_cols]) * both[:, hidden_cols:]).astype(jnp.bfloat16)
    return middle + project_rows(hidden, w_down)


def solution(mesh):
    placed = (
        P("tensor", ("group", "dp")),
        P(("group", "dp")),
        P(("group", "dp")),
        P(("group", "dp"), "tensor"),
        P(("group", "dp"), "tensor"),
        P("tensor", ("group", "dp")),
        P(("group", "dp"), "tensor"),
        P(("group", "dp"), "tensor"),
        P("tensor", ("group", "dp")),
        P(("group", "dp"), "tensor", None, None),
        P(("group", "dp")),
        P(("group", "dp")),
    )
    return jax.shard_map(
        per_device,
        mesh=mesh,
        in_specs=placed,
        out_specs=P("tensor", ("group", "dp")),
        check_vma=False,
    )
```

profile of v0, /device:TPU:6, one launch (start us, length us, event | category | flops | bytes accessed | tf_op | source)
XLA Modules:
  0.0 643.8 jit_solution(16838073562884392161)
XLA Ops:
  6.5 1.0 fusion.11
  7.6 62.1 %psum.14 = f32[64]{0:T(128)S(1)} all-reduce(f32[64]{0:T(128)S(1)} %fusion.11), channel_id=1, replica_groups=mesh['group'=2,'dp'=16,'tensor'=8] {'group','dp'}, use_global_device_ids=true, to_apply=%region_2.0 | all-reduce | flops 64 | bytes 512 | tf_op jit(solution)/shard_map/psum | solution.py:12
  71.1 26.8 %all_gather.12 = bf16[512,256]{1,0:T(8,128)(2,1)S(1)} all-gather(bf16[64,256]{1,0:T(8,128)(2,1)S(1)} %fusion.13), channel_id=1, replica_groups=mesh['group'=2,'dp'=16,'tensor'=8] {'tensor'}, dimensions={0}, use_global_device_ids=true | all-gather | bytes 294912 | tf_op jit(solution)/shard_map/all_gather | solution.py:18
  98.0 1.1 fusion.33
  99.1 1.5 fusion.32
  100.6 1.7 pad_maximum_fusion.1
  103.1 15.8 %all_to_all.24 = s32[32,1,2]{2,1,0:T(1,128)S(1)} all-to-all(s32[32,1,2]{2,1,0:T(1,128)S(1)} %bitcast.51), channel_id=1, replica_groups=mesh['group'=2,'dp'=16,'tensor'=8] {'group','dp'}, dimensions={0} | all-to-all | bytes 512 | tf_op jit(solution)/shard_map/all_to_all | solution.py:116
  121.1 69.7 %reduce-scatter.5.cloned.1.call-done = f32[16,1280]{1,0:T(8,128)} async-done(((f32[512,1280]{1,0:T(8,128)}), f32[16,1280]{1,0:T(8,128)}) %reduce-scatter.5.cloned.1.call-update) | async-done | bytes 81936 | tf_op jit(solution)/shard_map/reduce_scatter | solution.py:19
  193.0 5.9 all-to-all-start.2
  199.0 5.3 gather_fusion.1
  205.8 7.4 %all-to-all-start.1 = ((bf16[32,2,1024]{2,1,0:T(2,128)(2,1)}), bf16[32,2,1024]{2,1,0:T(2,128)(2,1)S(1)}, u32[]{:S(2)}, u32[]{:S(2)}) async-start(bf16[32,2,1024]{2,1,0:T(2,128)(2,1)} %reshape.144), calls=%async_computation.2 | async-start | bytes 262144 | tf_op jit(solution)/shard_map/all_to_all | solution.py:114
  213.2 6.3 all-to-all-done.1
  219.8 3.5 select_reduce_fusion
  223.6 3.0 fusion.4
  227.3 5.2 all-to-all-start.3
  232.6 6.4 all-to-all-done.3
  239.0 1.2 gather_fusion.2
  240.3 46.3 %all-gather.6.cloned.1.call-done = bf16[512,1024]{1,0:T(8,128)(2,1)} async-done(((bf16[16,1024]{1,0:T(8,128)(2,1)}), bf16[512,1024]{1,0:T(8,128)(2,1)}) %all-gather.6.cloned.1.call-update) | async-done | bytes 1048592 | tf_op jit(solution)/shard_map/all_gather | solution.py:32
  286.6 2.5 fusion.34
  289.2 37.6 %reduce-scatter.7.cloned.1.call-done = f32[64,256]{1,0:T(8,128)} async-done(((f32[512,256]{1,0:T(8,128)}), f32[64,256]{1,0:T(8,128)}) %reduce-scatter.7.cloned.1.call-update) | async-done | bytes 65552 | tf_op jit(solution)/shard_map/reduce_scatter | solution.py:36
  326.8 0.9 multiply_reduce_fusion
  327.7 60.4 %psum.15 = f32[64]{0:T(128)S(1)} all-reduce(f32[64]{0:T(128)S(1)} %multiply_reduce_fusion), channel_id=1, replica_groups=mesh['group'=2,'dp'=16,'tensor'=8] {'group','dp'}, use_global_device_ids=true, to_apply=%region_10.11 | all-reduce | flops 64 | bytes 512 | tf_op jit(solution)/shard_map/psum | solution.py:12
  389.1 24.9 %all_gather.14 = bf16[512,256]{1,0:T(8,128)(2,1)S(1)} all-gather(bf16[64,256]{1,0:T(8,128)(2,1)S(1)} %multiply_convert_fusion), channel_id=1, replica_groups=mesh['group'=2,'dp'=16,'tensor'=8] {'tensor'}, dimensions={0}, use_global_device_ids=true | all-gather | bytes 294912 | tf_op jit(solution)/shard_map/all_gather | solution.py:18
  414.0 2.8 fusion.36
  416.7 1.1 fusion.35
  417.8 5.5 pad_maximum_fusion
  423.4 117.5 %reduce-scatter.9.cloned.1.call-done = f32[16,7168]{1,0:T(8,128)} async-done(((f32[512,7168]{1,0:T(8,128)}), f32[16,7168]{1,0:T(8,128)}) %reduce-scatter.9.cloned.1.call-update) | async-done | bytes 458768 | tf_op jit(solution)/shard_map/reduce_scatter | solution.py:19
  540.9 1.8 fusion.10
  542.7 50.4 %all-gather.4.cloned.1.call-done = bf16[512,3584]{1,0:T(8,128)(2,1)} async-done(((bf16[16,3584]{1,0:T(8,128)(2,1)}), bf16[512,3584]{1,0:T(8,128)(2,1)}) %all-gather.4.cloned.1.call-update) | async-done | bytes 3670032 | tf_op jit(solution)/shard_map/all_gather | solution.py:32
  593.1 4.5 fusion.37
  597.7 37.7 %reduce-scatter.11.cloned.1.call-done = f32[64,256]{1,0:T(8,128)} async-done(((f32[512,256]{1,0:T(8,128)}), f32[64,256]{1,0:T(8,128)}) %reduce-scatter.11.cloned.1.call-update) | async-done | bytes 65552 | tf_op jit(solution)/shard_map/reduce_scatter | solution.py:36
  635.4 1.5 fusion.19
  (60 shorter events, 10.7 us)
Async XLA Ops:
  6.5 192.5 %copy-start = (bf16[16,1,256,256]{3,2,1,0:T(8,128)(2,1)S(1)}, bf16[16,1,256,256]{3,2,1,0:T(8,128)(2,1)}, u32[]{:S(2)}) copy-start(bf16[16,1,256,256]{3,2,1,0:T(8,128)(2,1)} %param.21) | copy-start | bytes 6291460
  6.5 184.3 %reduce-scatter.5.cloned.1.call-start = ((), (), s32[]{:S(2)}) async-start(), calls=%async_computation.8 | async-start | bytes 2703360 | tf_op jit(solution)/shard_map/reduce_scatter | solution.py:19
  100.6 1.8 copy-start.6
  100.6 19.7 %copy-start.1 = (s32[16]{0:T(128)S(1)}, s32[16]{0:T(128)}, u32[]{:S(2)}) copy-start(s32[16]{0:T(128)} %param.22) | copy-start | bytes 196
  193.0 12.8 %all-to-all-start.2 = ((bf16[32,2,256]{2,1,0:T(2,128)(2,1)}), bf16[32,2,256]{2,1,0:T(2,128)(2,1)S(1)}, u32[]{:S(2)}, u32[]{:S(2)}) async-start(bf16[32,2,256]{2,1,0:T(2,128)(2,1)} %reshape.147), calls=%async_computation.3 | async-start | bytes 65536 | tf_op jit(solution)/shard_map/all_to_all | solution.py:115
  205.8 13.7 %all-to-all-start.1 = ((bf16[32,2,1024]{2,1,0:T(2,128)(2,1)}), bf16[32,2,1024]{2,1,0:T(2,128)(2,1)S(1)}, u32[]{:S(2)}, u32[]{:S(2)}) async-start(bf16[32,2,1024]{2,1,0:T(2,128)(2,1)} %reshape.144), calls=%async_computation.2 | async-start | bytes 262144 | tf_op jit(solution)/shard_map/all_to_all | solution.py:114
  223.6 63.0 %copy-start.5 = (bf16[1024,256]{1,0:T(8,128)(2,1)S(1)}, bf16[1024,256]{1,0:T(8,128)(2,1)}, u32[]{:S(2)}) copy-start(bf16[1024,256]{1,0:T(8,128)(2,1)} %param.17) | copy-start | bytes 1572868
  223.6 65.6 %copy-start.7 = (bf16[256]{0:T(256)(128)(2,1)S(1)}, bf16[256]{0:T(256)(128)(2,1)}, u32[]{:S(2)}) copy-start(bf16[256]{0:T(256)(128)(2,1)} %param.14) | copy-start | bytes 1540
  223.6 103.2 %copy-start.3 = (bf16[64,256]{1,0:T(8,128)(2,1)S(1)}, bf16[64,256]{1,0:T(8,128)(2,1)}, u32[]{:S(2)}) copy-start(bf16[64,256]{1,0:T(8,128)(2,1)} %param.12) | copy-start | bytes 98308
  227.3 11.7 %all-to-all-start.3 = ((bf16[32,2,1024]{2,1,0:T(2,128)(2,1)}), bf16[32,2,1024]{2,1,0:T(2,128)(2,1)S(1)}, u32[]{:S(2)}, u32[]{:S(2)}) async-start(bf16[32,2,1024]{2,1,0:T(2,128)(2,1)} %convert_element_type.59), calls=%async_computation.4 | async-start | bytes 262144 | tf_op jit(solution)/shard_map/all_to_all | solution.py:127
  232.5 54.0 %all-gather.6.cloned.1.call-start = ((), (), s32[]{:S(2)}) async-start(), calls=%async_computation.13 | async-start | bytes 1081344 | tf_op jit(solution)/shard_map/all_gather | solution.py:32
  240.3 86.5 %reduce-scatter.7.cloned.1.call-start = ((), (), s32[]{:S(2)}) async-start(), calls=%async_computation.9 | async-start | bytes 589824 | tf_op jit(solution)/shard_map/reduce_scatter | solution.py:36
  289.1 251.8 %reduce-scatter.9.cloned.1.call-start = ((), (), s32[]{:S(2)}) async-start(), calls=%async_computation.10 | async-start | bytes 15138816 | tf_op jit(solution)/shard_map/reduce_scatter | solution.py:19
  414.0 2.8 copy-start.2
  423.4 169.8 %all-gather.4.cloned.1.call-start = ((), (), s32[]{:S(2)}) async-start(), calls=%async_computation.11 | async-start | bytes 3784704 | tf_op jit(solution)/shard_map/all_gather | solution.py:32
  542.7 92.8 %copy-start.4 = (f32[64,256]{1,0:T(8,128)S(1)}, f32[64,256]{1,0:T(8,128)}, u32[]{:S(2)}) copy-start(f32[64,256]{1,0:T(8,128)} %reduce-scatter.7.cloned.1.call-done) | copy-start | bytes 196612
  542.7 92.8 %reduce-scatter.11.cloned.1.call-start = ((), (), s32[]{:S(2)}) async-start(), calls=%async_computation.12 | async-start | bytes 589824 | tf_op jit(solution)/shard_map/reduce_scatter | solution.py:36
Sparse Core Ops, SparseCore 0:
  102.5 88.2 reduce-scatter.4
  240.4 46.1 all-gather.5
  289.2 37.5 reduce-scatter.6
  423.5 117.3 reduce-scatter.8
  543.3 49.8 all-gather.3
  597.8 37.5 reduce-scatter.10
where the time goes:
time: 645 us; the launch traced here: 644 us
  waiting for transfers between devices  372 us (58%)
  blocking collectives  190 us (29%)
  matrix products  20.1 us (3%)
  starting transfers between devices  18.7 us (3%)
  other arithmetic  16.8 us (3%)
  between operations  13.8 us (2%)
  local copies, waits for them, and re-layouts  12.3 us (2%)
    reduce_scatter x2, waiting for transfers between devices, width_sum(): lax.psum_scatter(jnp.concatenate([jnp.dot(gathered, matrix, preferred_ele...  187 us
    psum x2, blocking collectives, normed(): squares = lax.psum(jnp.sum(values * values, axis=1), ('group', 'dp'))  123 us
    all_gather x2, waiting for transfers between devices, project_rows(): lax.all_gather(local_rows, ('group', 'dp'), axis=0, tiled=True)  96.7 us
    reduce_scatter x2, waiting for transfers between devices, project_rows(): lax.psum_scatter(partial_sum, 'tensor', scatter_dimension=0, tiled=True)  75.4 us
    all_gather x2, blocking collectives, width_sum(): gathered = lax.all_gather(normal_rows, 'tensor', axis=0, tiled=True)  51.7 us
    all_to_all x1, blocking collectives, per_device(): lax.all_to_all(send_slot, ('group', 'dp'), split_axis=0, concat_axis=0, t...  15.8 us
  transfers between devices with their start and end apart: 9, of which 8 were waited for; matrix products, arithmetic and copies ran while one was open for 1% of the time, Pallas kernels for 0%

commit v1 on v0

--- a/solution.py
+++ b/solution.py
@@ -15,7 +15,9 @@
 
 
 def width_sum(normal_rows, matrices):
-    gathered = lax.all_gather(normal_rows, "tensor", axis=0, tiled=True)
+    gathered = jnp.concatenate(
+        lax.all_to_all(jnp.stack([normal_rows] * lax.axis_size("tensor")), "tensor", 0, 0), axis=0
+    )
     return lax.psum_scatter(
         jnp.concatenate(
             [jnp.dot(gathered, matrix, preferred_element_type=jnp.float32) for matrix in matrices],

time: 645 us -> 621 us (0.963)
  blocking collectives: 190 us -> 172 us
    all_gather x2 -> x0, blocking collectives: 51.7 us -> none  [width_sum(): gathered = lax.all_gather(normal_rows, 'tensor', axis=0, tiled=True)]
    all_to_all x0 -> x2, blocking collectives: none -> 31.8 us  [width_sum(): lax.all_to_all(jnp.stack([normal_rows] * lax.axis_size('tensor')), 'tenso...]
  transfers between devices with their start and end apart: 9 -> 9, of which waited for: 8 -> 8; matrix products, arithmetic and copies ran while one was open for 1% -> 2% of each run, Pallas kernels for 0% -> 0%
where the time goes in v1:
time: 621 us; the launch traced here: 620 us
  waiting for transfers between devices  367 us (59%)
  blocking collectives  172 us (28%)
  matrix products  20.1 us (3%)
  starting transfers between devices  18.7 us (3%)
  other arithmetic  16.8 us (3%)
  between operations  13.8 us (2%)
  local copies, waits for them, and re-layouts  12.3 us (2%)
    reduce_scatter x2, waiting for transfers between devices, width_sum(): lax.psum_scatter(jnp.concatenate([jnp.dot(gathered, matrix, preferred_ele...  182 us
    psum x2, blocking collectives, normed(): squares = lax.psum(jnp.sum(values * values, axis=1), ('group', 'dp'))  123 us
    all_gather x2, waiting for transfers between devices, project_rows(): lax.all_gather(local_rows, ('group', 'dp'), axis=0, tiled=True)  96.7 us
    reduce_scatter x2, waiting for transfers between devices, project_rows(): lax.psum_scatter(partial_sum, 'tensor', scatter_dimension=0, tiled=True)  75.4 us
    all_to_all x2, blocking collectives, width_sum(): lax.all_to_all(jnp.stack([normal_rows] * lax.axis_size('tensor')), 'tenso...  31.8 us
    all_to_all x1, blocking collectives, per_device(): lax.all_to_all(send_slot, ('group', 'dp'), split_axis=0, concat_axis=0, t...  17.7 us
  transfers between devices with their start and end apart: 9, of which 8 were waited for; matrix products, arithmetic and copies ran while one was open for 2% of the time, Pallas kernels for 0%

profile of v1, /device:TPU:6, one launch (start us, length us, event | category | flops | bytes accessed | tf_op | source)
XLA Modules:
  0.0 620.3 jit_solution(16713877027920137040)
XLA Ops:
  6.5 1.0 fusion.11
  7.6 62.1 %psum.14 = f32[64]{0:T(128)S(1)} all-reduce(f32[64]{0:T(128)S(1)} %fusion.11), channel_id=1, replica_groups=mesh['group'=2,'dp'=16,'tensor'=8] {'group','dp'}, use_global_device_ids=true, to_apply=%region_2.0 | all-reduce | flops 64 | bytes 512 | tf_op jit(solution)/shard_map/psum | solution.py:12
  71.2 17.3 %all_to_all.34 = bf16[8,64,256]{2,1,0:T(8,128)(2,1)S(1)} all-to-all(bf16[8,64,256]{2,1,0:T(8,128)(2,1)S(1)} %stack.4), channel_id=1, replica_groups=mesh['group'=2,'dp'=16,'tensor'=8] {'tensor'}, dimensions={0} | all-to-all | bytes 524288 | tf_op jit(solution)/shard_map/all_to_all | solution.py:19
  88.5 1.1 fusion.33
  89.6 1.5 fusion.32
  91.1 1.7 pad_maximum_fusion.1
  93.6 17.7 %all_to_all.35 = s32[32,1,2]{2,1,0:T(1,128)S(1)} all-to-all(s32[32,1,2]{2,1,0:T(1,128)S(1)} %bitcast.57), channel_id=1, replica_groups=mesh['group'=2,'dp'=16,'tensor'=8] {'group','dp'}, dimensions={0} | all-to-all | bytes 512 | tf_op jit(solution)/shard_map/all_to_all | solution.py:118
  113.4 66.7 %reduce-scatter.5.cloned.1.call-done = f32[16,1280]{1,0:T(8,128)} async-done(((f32[512,1280]{1,0:T(8,128)}), f32[16,1280]{1,0:T(8,128)}) %reduce-scatter.5.cloned.1.call-update) | async-done | bytes 81936 | tf_op jit(solution)/shard_map/reduce_scatter | solution.py:21
  182.3 5.8 all-to-all-start.3
  188.3 5.3 gather_fusion.1
  195.1 7.4 %all-to-all-start.2 = ((bf16[32,2,1024]{2,1,0:T(2,128)(2,1)}), bf16[32,2,1024]{2,1,0:T(2,128)(2,1)S(1)}, u32[]{:S(2)}, u32[]{:S(2)}) async-start(bf16[32,2,1024]{2,1,0:T(2,128)(2,1)} %reshape.155), calls=%async_computation.3 | async-start | bytes 262144 | tf_op jit(solution)/shard_map/all_to_all | solution.py:116
  202.5 6.3 %all-to-all-done.2 = bf16[32,2,1024]{2,1,0:T(2,128)(2,1)S(1)} async-done(((bf16[32,2,1024]{2,1,0:T(2,128)(2,1)}), bf16[32,2,1024]{2,1,0:T(2,128)(2,1)S(1)}, u32[]{:S(2)}, u32[]{:S(2)}) %all-to-all-start.2) | async-done | bytes 131104 | tf_op jit(solution)/shard_map/all_to_all | solution.py:116
  209.1 3.5 select_reduce_fusion
  212.9 3.0 fusion.4
  216.6 5.2 all-to-all-start.4
  221.9 6.4 %all-to-all-done.4 = bf16[32,2,1024]{2,1,0:T(2,128)(2,1)S(1)} async-done(((bf16[32,2,1024]{2,1,0:T(2,128)(2,1)}), bf16[32,2,1024]{2,1,0:T(2,128)(2,1)S(1)}, u32[]{:S(2)}, u32[]{:S(2)}) %all-to-all-start.4) | async-done | bytes 131104 | tf_op jit(solution)/shard_map/all_to_all | solution.py:129
  228.3 1.2 gather_fusion.2
  229.6 46.3 %all-gather.6.cloned.1.call-done = bf16[512,1024]{1,0:T(8,128)(2,1)} async-done(((bf16[16,1024]{1,0:T(8,128)(2,1)}), bf16[512,1024]{1,0:T(8,128)(2,1)}) %all-gather.6.cloned.1.call-update) | async-done | bytes 1048592 | tf_op jit(solution)/shard_map/all_gather | solution.py:34
  275.9 2.5 fusion.34
  278.4 37.6 %reduce-scatter.7.cloned.1.call-done = f32[64,256]{1,0:T(8,128)} async-done(((f32[512,256]{1,0:T(8,128)}), f32[64,256]{1,0:T(8,128)}) %reduce-scatter.7.cloned.1.call-update) | async-done | bytes 65552 | tf_op jit(solution)/shard_map/reduce_scatter | solution.py:38
  316.1 0.9 multiply_reduce_fusion
  317.0 60.4 %psum.15 = f32[64]{0:T(128)S(1)} all-reduce(f32[64]{0:T(128)S(1)} %multiply_reduce_fusion), channel_id=1, replica_groups=mesh['group'=2,'dp'=16,'tensor'=8] {'group','dp'}, use_global_device_ids=true, to_apply=%region_10.11 | all-reduce | flops 64 | bytes 512 | tf_op jit(solution)/shard_map/psum | solution.py:12
  378.4 14.5 %all_to_all.36 = bf16[8,64,256]{2,1,0:T(8,128)(2,1)S(1)} all-to-all(bf16[8,64,256]{2,1,0:T(8,128)(2,1)S(1)} %stack.5), channel_id=1, replica_groups=mesh['group'=2,'dp'=16,'tensor'=8] {'tensor'}, dimensions={0} | all-to-all | bytes 524288 | tf_op jit(solution)/shard_map/all_to_all | solution.py:19
  392.9 2.7 fusion.36
  395.7 1.1 fusion.35
  396.8 5.5 pad_maximum_fusion
  402.4 115.1 %reduce-scatter.9.cloned.1.call-done = f32[16,7168]{1,0:T(8,128)} async-done(((f32[512,7168]{1,0:T(8,128)}), f32[16,7168]{1,0:T(8,128)}) %reduce-scatter.9.cloned.1.call-update) | async-done | bytes 458768 | tf_op jit(solution)/shard_map/reduce_scatter | solution.py:21
  517.5 1.8 fusion.10
  519.3 50.4 %all-gather.4.cloned.1.call-done = bf16[512,3584]{1,0:T(8,128)(2,1)} async-done(((bf16[16,3584]{1,0:T(8,128)(2,1)}), bf16[512,3584]{1,0:T(8,128)(2,1)}) %all-gather.4.cloned.1.call-update) | async-done | bytes 3670032 | tf_op jit(solution)/shard_map/all_gather | solution.py:34
  569.7 4.5 fusion.37
  574.2 37.7 %reduce-scatter.11.cloned.1.call-done = f32[64,256]{1,0:T(8,128)} async-done(((f32[512,256]{1,0:T(8,128)}), f32[64,256]{1,0:T(8,128)}) %reduce-scatter.11.cloned.1.call-update) | async-done | bytes 65552 | tf_op jit(solution)/shard_map/reduce_scatter | solution.py:38
  612.0 1.5 fusion.19
  (62 shorter events, 10.7 us)
Async XLA Ops:
  6.5 181.7 %copy-start = (bf16[16,1,256,256]{3,2,1,0:T(8,128)(2,1)S(1)}, bf16[16,1,256,256]{3,2,1,0:T(8,128)(2,1)}, u32[]{:S(2)}) copy-start(bf16[16,1,256,256]{3,2,1,0:T(8,128)(2,1)} %param.21) | copy-start | bytes 6291460
  6.5 173.6 %reduce-scatter.5.cloned.1.call-start = ((), (), s32[]{:S(2)}) async-start(), calls=%async_computation.10 | async-start | bytes 2703360 | tf_op jit(solution)/shard_map/reduce_scatter | solution.py:21
  91.1 1.8 copy-start.6
  91.1 21.5 %copy-start.1 = (s32[16]{0:T(128)S(1)}, s32[16]{0:T(128)}, u32[]{:S(2)}) copy-start(s32[16]{0:T(128)} %param.22) | copy-start | bytes 196
  182.3 12.7 %all-to-all-start.3 = ((bf16[32,2,256]{2,1,0:T(2,128)(2,1)}), bf16[32,2,256]{2,1,0:T(2,128)(2,1)S(1)}, u32[]{:S(2)}, u32[]{:S(2)}) async-start(bf16[32,2,256]{2,1,0:T(2,128)(2,1)} %reshape.158), calls=%async_computation.4 | async-start | bytes 65536 | tf_op jit(solution)/shard_map/all_to_all | solution.py:117
  195.1 13.7 %all-to-all-start.2 = ((bf16[32,2,1024]{2,1,0:T(2,128)(2,1)}), bf16[32,2,1024]{2,1,0:T(2,128)(2,1)S(1)}, u32[]{:S(2)}, u32[]{:S(2)}) async-start(bf16[32,2,1024]{2,1,0:T(2,128)(2,1)} %reshape.155), calls=%async_computation.3 | async-start | bytes 262144 | tf_op jit(solution)/shard_map/all_to_all | solution.py:116
  212.9 63.0 %copy-start.5 = (bf16[1024,256]{1,0:T(8,128)(2,1)S(1)}, bf16[1024,256]{1,0:T(8,128)(2,1)}, u32[]{:S(2)}) copy-start(bf16[1024,256]{1,0:T(8,128)(2,1)} %param.17) | copy-start | bytes 1572868
  212.9 65.6 %copy-start.7 = (bf16[256]{0:T(256)(128)(2,1)S(1)}, bf16[256]{0:T(256)(128)(2,1)}, u32[]{:S(2)}) copy-start(bf16[256]{0:T(256)(128)(2,1)} %param.14) | copy-start | bytes 1540
  212.9 103.2 %copy-start.3 = (bf16[64,256]{1,0:T(8,128)(2,1)S(1)}, bf16[64,256]{1,0:T(8,128)(2,1)}, u32[]{:S(2)}) copy-start(bf16[64,256]{1,0:T(8,128)(2,1)} %param.12) | copy-start | bytes 98308
  216.6 11.7 %all-to-all-start.4 = ((bf16[32,2,1024]{2,1,0:T(2,128)(2,1)}), bf16[32,2,1024]{2,1,0:T(2,128)(2,1)S(1)}, u32[]{:S(2)}, u32[]{:S(2)}) async-start(bf16[32,2,1024]{2,1,0:T(2,128)(2,1)} %convert_element_type.59), calls=%async_computation.5 | async-start | bytes 262144 | tf_op jit(solution)/shard_map/all_to_all | solution.py:129
  221.8 54.0 %all-gather.6.cloned.1.call-start = ((), (), s32[]{:S(2)}) async-start(), calls=%async_computation.15 | async-start | bytes 1081344 | tf_op jit(solution)/shard_map/all_gather | solution.py:34
  229.5 86.5 %reduce-scatter.7.cloned.1.call-start = ((), (), s32[]{:S(2)}) async-start(), calls=%async_computation.11 | async-start | bytes 589824 | tf_op jit(solution)/shard_map/reduce_scatter | solution.py:38
  278.4 239.1 %reduce-scatter.9.cloned.1.call-start = ((), (), s32[]{:S(2)}) async-start(), calls=%async_computation.12 | async-start | bytes 15138816 | tf_op jit(solution)/shard_map/reduce_scatter | solution.py:21
  392.9 2.8 copy-start.2
  402.3 167.3 %all-gather.4.cloned.1.call-start = ((), (), s32[]{:S(2)}) async-start(), calls=%async_computation.13 | async-start | bytes 3784704 | tf_op jit(solution)/shard_map/all_gather | solution.py:34
  519.2 92.7 %copy-start.4 = (f32[64,256]{1,0:T(8,128)S(1)}, f32[64,256]{1,0:T(8,128)}, u32[]{:S(2)}) copy-start(f32[64,256]{1,0:T(8,128)} %reduce-scatter.7.cloned.1.call-done) | copy-start | bytes 196612
  519.2 92.7 %reduce-scatter.11.cloned.1.call-start = ((), (), s32[]{:S(2)}) async-start(), calls=%async_computation.14 | async-start | bytes 589824 | tf_op jit(solution)/shard_map/reduce_scatter | solution.py:38
Sparse Core Ops, SparseCore 0:
  93.0 87.1 reduce-scatter.4
  229.7 46.1 all-gather.5
  278.5 37.5 reduce-scatter.6
  402.5 114.9 reduce-scatter.8
  519.8 49.7 all-gather.3
  574.4 37.5 reduce-scatter.10
